TPU v7x, 256 devices: a whole 4x4x8 slice. The times are simulated.
256 devices in a mesh: ta: 8 (over x_lo, y), gx: 4 (over x_hi, core), yz: 8 (over z).
Axes of the slice: x: 4 (x_hi: 2, x_lo: 2; x = x_hi * 2 + x_lo), y: 4, z: 8, core: 2. Of those that a mesh axis runs over, the one named last changes fastest.
Arguments:
- vectors: bfloat16 [2, 3, 32, 64, 256, 128], P(None, None, 'gx', 'yz', 'ta'), parts along dimension 4, may hold values from -6 to 6
- gauge_x: float32 [2, 3, 3, 32, 64, 256], P(None, None, None, 'gx', 'yz', 'ta'), parts along dimension 5, may hold values from -6 to 6
- gauge_y: float32 [2, 3, 3, 32, 64, 256], P(None, None, None, 'gx', 'yz', 'ta'), parts along dimension 5, may hold values from -6 to 6
Outputs:
- elementals: float32 [16, 2, 128, 128], P('ta'), parts along dimension 0
There are 8 independent parts, one for each index of `ta`. A program takes and returns all parts, laid end to end along the dimension named above; each array names one. Nothing has to cross between parts.
All inputs are finite; a program needn't handle non-finite values.
Results may differ from a plain program's by a relative error of at most 0.0029.
Values may be sent and summed in bfloat16 or wider, within the bound.
No kernel may reach another device: no remote copies, remote signals or barrier semaphores. Data moves between devices by JAX's collectives and lax.ppermute only.
A program may use at most 64 MiB of HBM per device.

v0:
```python
import math
import jax
import jax.numpy as jnp
from jax import lax
from jax.sharding import PartitionSpec as P


def shifted(value, axis, steps):
    count = lax.axis_size(axis)
    pairs = [(source, (source + steps) % count) for source in range(count)]
    return lax.ppermute(value, axis, pairs)


def colour_apply(gauge, source_vectors):
    real_parts = []
    imag_parts = []
    for colour in range(3):
        real_running = jnp.zeros(source_vectors.shape[2:], jnp.float32)
        imaginary_running = jnp.zeros(source_vectors.shape[2:], jnp.float32)
        for inner_product in range(3):
            left_real = gauge[0, colour, inner_product][..., None]
            left_imaginary = gauge[1, colour, inner_product][..., None]
            right_real = source_vectors[0, inner_product].astype(jnp.float32)
            right_imaginary = source_vectors[1, inner_product].astype(jnp.float32)
            real_running = real_running + left_real * right_real - left_imaginary * right_imaginary
            imaginary_running = (
                imaginary_running + left_real * right_imaginary + left_imaginary * right_real
            )
        real_parts.append(real_running)
        imag_parts.append(imaginary_running)
    return jnp.stack([jnp.stack(real_parts), jnp.stack(imag_parts)]).astype(jnp.bfloat16)


def right_block(image):
    nvecs = image.shape[-1]
    real_rows = image[0].reshape(-1, nvecs)
    imag_rows = image[1].reshape(-1, nvecs)
    first = jnp.concatenate([real_rows, imag_rows], 0)
    second = jnp.concatenate([imag_rows, -real_rows], 0)
    return (first, second)


def contract(left_cols, right_cols):
    return lax.dot_general(
        left_cols, right_cols, (((0,), (0,)), ((), ())), preferred_element_type=jnp.float32
    )


def local(vectors, gauge_x, gauge_y):
    nvecs = vectors.shape[-1]
    from_next_x = shifted(vectors[:, :, :1], "gx", -1)
    shifted_x = jnp.concatenate([vectors[:, :, 1:], from_next_x], 2)
    from_next_y = shifted(vectors[:, :, :, :1], "yz", -1)
    shifted_y = jnp.concatenate([vectors[:, :, :, 1:], from_next_y], 3)
    image_x = colour_apply(gauge_x, shifted_x)
    image_y = colour_apply(gauge_y, shifted_y)
    left_rows = vectors.reshape(-1, nvecs)
    blocks = right_block(image_x) + right_block(image_y)
    summed = lax.psum(
        jnp.concatenate([contract(left_rows, member) for member in blocks], 1), ("gx", "yz")
    )
    sites_total = (
        vectors.shape[2]
        * lax.axis_size("gx")
        * vectors.shape[3]
        * lax.axis_size("yz")
        * vectors.shape[4]
    )
    scaling = 1.0 / math.sqrt(3.0 * sites_total)
    return (summed * scaling).reshape(nvecs, 2, 2, nvecs).transpose(1, 2, 0, 3)


def solution(mesh):
    placed = (
        P(None, None, "gx", "yz", "ta", None),
        P(None, None, None, "gx", "yz", "ta"),
        P(None, None, None, "gx", "yz", "ta"),
    )
    return jax.shard_map(
        local, mesh=mesh, in_specs=placed, out_specs=P("ta", None, None, None), check_vma=False
    )
```

profile of v0, /device:TPU:8, one launch (start us, length us, event | category | flops | bytes accessed | tf_op | source)
XLA Modules:
  0.0 315.3 jit_solution(16234775033811610859)
XLA Ops:
  6.5 1.0 slice.186
  7.6 2.5 collective-permute-start
  10.1 1.0 slice.212
  11.1 5.9 %collective-permute-start.1 = (bf16[2,3,8,1,32,128]{5,4,3,2,1,0:T(8,128)(2,1)S(1)}, bf16[2,3,8,1,32,128]{5,4,3,2,1,0:T(8,128)(2,1)S(1)}, u32[]{:S(2)}, u32[]{:S(2)}) collective-permute-start(bf16[2,3,8,1,32,128]{5,4,3,2,1,0:T(8,128)(2,1)S(1)} %slice.212), channel_id=1, source_target_pairs={{0,7},{1,0},{2,1},{3,2},{4,3},{5,4},{6,5},{7,6},{8,15},{9,8},{10,9... | collective-permute-start | bytes 1179656 | tf_op jit(solution)/shard_map/ppermute | solution.py:11
  17.1 0.7 slice.211
  17.8 0.4 copy-done.1
  18.4 0.8 slice-done
  19.2 2.1 fusion.51
  21.3 1.9 fusion.33
  23.3 3.9 %fusion.57 = (bf16[1,8,8,32,128]{4,3,2,1,0:T(8,128)(2,1)S(1)}, bf16[1,8,8,32,128]{4,3,2,1,0:T(8,128)(2,1)S(1)}, bf16[1,8,8,32,128]{4,3,2,1,0:T(8,128)(2,1)S(1)}, bf16[1,8,8,32,128]{4,3,2,1,0:T(8,128)(2,1)S(1)}) fusion(bf16[1,8,8,32,128]{4,3,2,1,0:T(8,128)(2,1)S(1)} %get-tuple-element.11, bf16[1,8,8,32,128]{4,3,2,1,0:T(8,128)(2,1)S(1)} %get-tuple-element.10, ...), kind=kLoop, calls=%fused_computation.145 | loop fusion | flops 14155776 | bytes 5341184 | tf_op jit(solution)/shard_map/convert.26
  27.2 0.3 pad_maximum_fusion
  27.5 0.3 bitcast_negate_fusion.1
  27.8 1.0 fusion.25
  28.9 1.0 fusion.22
  29.9 2.0 fusion.87
  31.9 1.9 fusion.69
  33.9 3.9 %fusion.93 = (bf16[1,8,8,32,128]{4,3,2,1,0:T(8,128)(2,1)S(1)}, bf16[1,8,8,32,128]{4,3,2,1,0:T(8,128)(2,1)S(1)}, bf16[1,8,8,32,128]{4,3,2,1,0:T(8,128)(2,1)S(1)}, bf16[1,8,8,32,128]{4,3,2,1,0:T(8,128)(2,1)S(1)}) fusion(bf16[1,8,8,32,128]{4,3,2,1,0:T(8,128)(2,1)S(1)} %get-tuple-element.18, bf16[1,8,8,32,128]{4,3,2,1,0:T(8,128)(2,1)S(1)} %get-tuple-element.17, ...), kind=kLoop, calls=%fused_computation.181 | loop fusion | flops 14155776 | bytes 5341184 | tf_op jit(solution)/shard_map/convert.16
  37.8 0.3 pad_maximum_fusion.2
  38.5 1.0 fusion.19
  39.5 1.1 fusion.16
  40.6 0.7 pad_maximum_fusion.6
  41.3 265.3 %all-reduce.2.cloned.1.call-done = f32[128,512]{0,1:T(8,128)} async-done(((f32[128,512]{0,1:T(8,128)}), f32[128,512]{0,1:T(8,128)}) %all-reduce.2.cloned.1.call-update) | async-done | bytes 262160 | tf_op jit(solution)/shard_map/psum | solution.py:59
  306.6 1.0 broadcast_multiply_fusion
  307.6 0.8 copy.4
  (13 shorter events, 0.6 us)
Async XLA Ops:
  6.5 300.1 %all-reduce.2.cloned.1.call-start = ((), (), s32[]{:S(2)}) async-start(), calls=%async_computation | async-start | bytes 524288 | tf_op jit(solution)/shard_map/psum | solution.py:59
  7.6 9.5 %copy-start = (bf16[2,3,8,8,32,128]{5,4,3,2,1,0:T(8,128)(2,1)S(1)}, bf16[2,3,8,8,32,128]{5,4,3,2,1,0:T(8,128)(2,1)}, u32[]{:S(2)}) copy-start(bf16[2,3,8,8,32,128]{5,4,3,2,1,0:T(8,128)(2,1)} %param.3) | copy-start | bytes 9437188
  7.6 10.8 %collective-permute-start = (bf16[2,3,1,8,32,128]{5,4,3,2,1,0:T(8,128)(2,1)S(1)}, bf16[2,3,1,8,32,128]{5,4,3,2,1,0:T(8,128)(2,1)S(1)}, u32[]{:S(2)}, u32[]{:S(2)}) collective-permute-start(bf16[2,3,1,8,32,128]{5,4,3,2,1,0:T(8,128)(2,1)S(1)} %slice.186), channel_id=1, source_target_pairs={{0,24},{8,0},{16,8},{24,16},{1,25},{9,1},{17,9},{25,17},{2,26},{10... | collective-permute-start | bytes 1179656 | tf_op jit(solution)/shard_map/ppermute | solution.py:11
  11.1 18.8 %collective-permute-start.1 = (bf16[2,3,8,1,32,128]{5,4,3,2,1,0:T(8,128)(2,1)S(1)}, bf16[2,3,8,1,32,128]{5,4,3,2,1,0:T(8,128)(2,1)S(1)}, u32[]{:S(2)}, u32[]{:S(2)}) collective-permute-start(bf16[2,3,8,1,32,128]{5,4,3,2,1,0:T(8,128)(2,1)S(1)} %slice.212), channel_id=1, source_target_pairs={{0,7},{1,0},{2,1},{3,2},{4,3},{5,4},{6,5},{7,6},{8,15},{9,8},{10,9... | collective-permute-start | bytes 1179656 | tf_op jit(solution)/shard_map/ppermute | solution.py:11
  17.1 1.1 copy-start.1
  17.1 1.2 copy-start.2
  17.1 2.1 slice-start
Sparse Core Ops, SparseCore 0:
  41.5 265.1 all-reduce.1
where the time goes:
time: 315 us
  waiting for transfers between devices  265 us (84%)
  other arithmetic  18.8 us (6%)
  between operations  13.6 us (4%)
  starting transfers between devices  8.47 us (3%)
  local copies, waits for them, and re-layouts  5 us (2%)
  matrix products  4.18 us (1%)
    psum x1, waiting for transfers between devices, local(): lax.psum(jnp.concatenate([contract(left_rows, member) for member in block...  265 us
    another operation x6, other arithmetic  15.8 us
    ppermute x2, starting transfers between devices, shifted(): return lax.ppermute(value, axis, pairs)  8.47 us
  transfers between devices with their start and end apart: 3, of which 1 were waited for; matrix products, arithmetic and copies ran while one was open for 4% of the time, Pallas kernels for 0%

commit v1 on v0

--- a/solution.py
+++ b/solution.py
@@ -57,7 +57,7 @@
     left_rows = vectors.reshape(-1, nvecs)
     blocks = right_block(image_x) + right_block(image_y)
     summed = lax.psum(
-        jnp.concatenate([contract(left_rows, member) for member in blocks], 1), ("gx", "yz")
+        lax.psum(jnp.concatenate([contract(left_rows, member) for member in blocks], 1), "yz"), "gx"
     )
     sites_total = (
         vectors.shape[2]

time: 315 us -> 171 us (0.54)
  waiting for transfers between devices: 265 us -> 119 us
    psum x1, waiting for transfers between devices: 265 us -> 72.1 us  [local(): lax.psum(jnp.concatenate([contract(left_rows, member) for member in block...]
    psum x0 -> x1, waiting for transfers between devices: none -> 46.9 us  [local(): lax.psum(lax.psum(jnp.concatenate([contract(left_rows, member) for member...]
  transfers between devices with their start and end apart: 3 -> 4, of which waited for: 1 -> 2; matrix products, arithmetic and copies ran while one was open for 4% -> 7% of each run, Pallas kernels for 0% -> 0%
where the time goes in v1:
time: 171 us; the launch traced here: 169 us
  waiting for transfers between devices  119 us (70%)
  other arithmetic  18.8 us (11%)
  between operations  13.6 us (8%)
  starting transfers between devices  8.52 us (5%)
  local copies, waits for them, and re-layouts  5 us (3%)
  matrix products  4.18 us (2%)
    psum x1, waiting for transfers between devices, local(): lax.psum(jnp.concatenate([contract(left_rows, member) for member in block...  72.1 us
    psum x1, waiting for transfers between devices, local(): lax.psum(lax.psum(jnp.concatenate([contract(left_rows, member) for member...  46.9 us
    another operation x6, other arithmetic  15.8 us
    ppermute x2, starting transfers between devices, shifted(): return lax.ppermute(value, axis, pairs)  8.47 us
    dot_general x4, matrix products, contract(): lax.dot_general(left_cols, right_cols, (((0,), (0,)), ((), ())), preferre...  4.18 us
  transfers between devices with their start and end apart: 4, of which 2 were waited for; matrix products, arithmetic and copies ran while one was open for 7% of the time, Pallas kernels for 0%

profile of v1, /device:TPU:8, one launch (start us, length us, event | category | flops | bytes accessed | tf_op | source)
XLA Modules:
  0.0 169.0 jit_solution(5933804391679605913)
XLA Ops:
  6.5 1.0 slice.186
  7.6 2.5 %collective-permute-start = (bf16[2,3,1,8,32,128]{5,4,3,2,1,0:T(8,128)(2,1)S(1)}, bf16[2,3,1,8,32,128]{5,4,3,2,1,0:T(8,128)(2,1)S(1)}, u32[]{:S(2)}, u32[]{:S(2)}) collective-permute-start(bf16[2,3,1,8,32,128]{5,4,3,2,1,0:T(8,128)(2,1)S(1)} %slice.186), channel_id=1, source_target_pairs={{0,24},{8,0},{16,8},{24,16},{1,25},{9,1},{17,9},{25,17},{2,26},{10... | collective-permute-start | bytes 1179656 | tf_op jit(solution)/shard_map/ppermute | solution.py:11
  10.1 1.0 slice.212
  11.1 5.9 %collective-permute-start.1 = (bf16[2,3,8,1,32,128]{5,4,3,2,1,0:T(8,128)(2,1)S(1)}, bf16[2,3,8,1,32,128]{5,4,3,2,1,0:T(8,128)(2,1)S(1)}, u32[]{:S(2)}, u32[]{:S(2)}) collective-permute-start(bf16[2,3,8,1,32,128]{5,4,3,2,1,0:T(8,128)(2,1)S(1)} %slice.212), channel_id=1, source_target_pairs={{0,7},{1,0},{2,1},{3,2},{4,3},{5,4},{6,5},{7,6},{8,15},{9,8},{10,9... | collective-permute-start | bytes 1179656 | tf_op jit(solution)/shard_map/ppermute | solution.py:11
  17.1 0.7 slice.211
  17.8 0.4 copy-done.1
  18.4 0.8 slice-done
  19.2 2.1 %fusion.51 = (bf16[1,8,8,32,128]{4,3,2,1,0:T(8,128)(2,1)S(1)}, bf16[1,8,8,32,128]{4,3,2,1,0:T(8,128)(2,1)S(1)}, bf16[1,8,8,32,128]{4,3,2,1,0:T(8,128)(2,1)S(1)},...) fusion(f32[8,8,32]{2,1,0:T(8,128)S(1)} %get-tuple-element.41, ...), kind=kLoop, calls=%fused_computation.139 | loop fusion | flops 6291456 | bytes 6864896 | tf_op jit(solution)/shard_map/convert.25
  21.3 1.9 %fusion.33 = bf16[1,8,8,32,128]{4,3,2,1,0:T(8,128)(2,1)S(1)} fusion(bf16[1,8,8,32,128]{4,3,2,1,0:T(8,128)(2,1)S(1)} %get-tuple-element.11, bf16[1,8,8,32,128]{4,3,2,1,0:T(8,128)(2,1)S(1)} %get-tuple-element.10, bf16[1,8,8,32,128]{4,3,2,1,0:T(8,128)(2,1)S(1)} %get-tuple-element.9, bf16[1,8,8,32,128]{4,3,2,1,0:T(8,128)(2,1)S(1)} %get-tuple-element.8, ...), kind=kLoop, calls=%fused_computation.121 | loop fusion | flops 4718592 | bytes 3719168 | tf_op jit(solution)/shard_map/convert.29
  23.3 3.9 %fusion.57 = (bf16[1,8,8,32,128]{4,3,2,1,0:T(8,128)(2,1)S(1)}, bf16[1,8,8,32,128]{4,3,2,1,0:T(8,128)(2,1)S(1)}, bf16[1,8,8,32,128]{4,3,2,1,0:T(8,128)(2,1)S(1)}, bf16[1,8,8,32,128]{4,3,2,1,0:T(8,128)(2,1)S(1)}) fusion(bf16[1,8,8,32,128]{4,3,2,1,0:T(8,128)(2,1)S(1)} %get-tuple-element.11, bf16[1,8,8,32,128]{4,3,2,1,0:T(8,128)(2,1)S(1)} %get-tuple-element.10, ...), kind=kLoop, calls=%fused_computation.145 | loop fusion | flops 14155776 | bytes 5341184 | tf_op jit(solution)/shard_map/convert.26
  27.2 0.3 pad_maximum_fusion
  27.8 1.0 fusion.25
  28.9 1.0 fusion.22
  29.9 2.0 %fusion.87 = (bf16[1,8,8,32,128]{4,3,2,1,0:T(8,128)(2,1)S(1)}, bf16[1,8,8,32,128]{4,3,2,1,0:T(8,128)(2,1)S(1)}, bf16[1,8,8,32,128]{4,3,2,1,0:T(8,128)(2,1)S(1)},...) fusion(f32[8,8,32]{2,1,0:T(8,128)S(1)} %get-tuple-element.59, ...), kind=kLoop, calls=%fused_computation.175 | loop fusion | flops 6291456 | bytes 6864896 | tf_op jit(solution)/shard_map/convert.15
  31.9 1.9 %fusion.69 = bf16[1,8,8,32,128]{4,3,2,1,0:T(8,128)(2,1)S(1)} fusion(bf16[1,8,8,32,128]{4,3,2,1,0:T(8,128)(2,1)S(1)} %get-tuple-element.18, bf16[1,8,8,32,128]{4,3,2,1,0:T(8,128)(2,1)S(1)} %get-tuple-element.17, bf16[1,8,8,32,128]{4,3,2,1,0:T(8,128)(2,1)S(1)} %get-tuple-element.16, bf16[1,8,8,32,128]{4,3,2,1,0:T(8,128)(2,1)S(1)} %get-tuple-element.15, ...), kind=kLoop, calls=%fused_computation.157 | loop fusion | flops 4718592 | bytes 3719168 | tf_op jit(solution)/shard_map/convert.19
  33.9 3.9 %fusion.93 = (bf16[1,8,8,32,128]{4,3,2,1,0:T(8,128)(2,1)S(1)}, bf16[1,8,8,32,128]{4,3,2,1,0:T(8,128)(2,1)S(1)}, bf16[1,8,8,32,128]{4,3,2,1,0:T(8,128)(2,1)S(1)}, bf16[1,8,8,32,128]{4,3,2,1,0:T(8,128)(2,1)S(1)}) fusion(bf16[1,8,8,32,128]{4,3,2,1,0:T(8,128)(2,1)S(1)} %get-tuple-element.18, bf16[1,8,8,32,128]{4,3,2,1,0:T(8,128)(2,1)S(1)} %get-tuple-element.17, ...), kind=kLoop, calls=%fused_computation.181 | loop fusion | flops 14155776 | bytes 5341184 | tf_op jit(solution)/shard_map/convert.16
  37.8 0.3 pad_maximum_fusion.2
  38.5 1.0 fusion.19
  39.5 1.1 fusion.16
  40.6 0.7 pad_maximum_fusion.6
  41.4 72.1 %all-reduce.3.cloned.1.call-done = f32[128,512]{0,1:T(8,128)} async-done(((f32[128,512]{0,1:T(8,128)}), f32[128,512]{0,1:T(8,128)}) %all-reduce.3.cloned.1.call-update) | async-done | bytes 262160 | tf_op jit(solution)/shard_map/psum | solution.py:60
  113.5 46.9 %all-reduce.5.cloned.1.call-done = f32[128,512]{0,1:T(8,128)} async-done(((f32[128,512]{0,1:T(8,128)}), f32[128,512]{0,1:T(8,128)}) %all-reduce.5.cloned.1.call-update) | async-done | bytes 262160 | tf_op jit(solution)/shard_map/psum | solution.py:59
  160.4 1.0 broadcast_multiply_fusion
  161.4 0.8 copy.4
  (16 shorter events, 0.9 us)
Async XLA Ops:
  6.5 106.9 %all-reduce.3.cloned.1.call-start = ((), (), s32[]{:S(2)}) async-start(), calls=%async_computation | async-start | bytes 524288 | tf_op jit(solution)/shard_map/psum | solution.py:60
  7.6 9.5 %copy-start = (bf16[2,3,8,8,32,128]{5,4,3,2,1,0:T(8,128)(2,1)S(1)}, bf16[2,3,8,8,32,128]{5,4,3,2,1,0:T(8,128)(2,1)}, u32[]{:S(2)}) copy-start(bf16[2,3,8,8,32,128]{5,4,3,2,1,0:T(8,128)(2,1)} %param.3) | copy-start | bytes 9437188
  7.6 10.8 %collective-permute-start = (bf16[2,3,1,8,32,128]{5,4,3,2,1,0:T(8,128)(2,1)S(1)}, bf16[2,3,1,8,32,128]{5,4,3,2,1,0:T(8,128)(2,1)S(1)}, u32[]{:S(2)}, u32[]{:S(2)}) collective-permute-start(bf16[2,3,1,8,32,128]{5,4,3,2,1,0:T(8,128)(2,1)S(1)} %slice.186), channel_id=1, source_target_pairs={{0,24},{8,0},{16,8},{24,16},{1,25},{9,1},{17,9},{25,17},{2,26},{10... | collective-permute-start | bytes 1179656 | tf_op jit(solution)/shard_map/ppermute | solution.py:11
  11.1 18.8 %collective-permute-start.1 = (bf16[2,3,8,1,32,128]{5,4,3,2,1,0:T(8,128)(2,1)S(1)}, bf16[2,3,8,1,32,128]{5,4,3,2,1,0:T(8,128)(2,1)S(1)}, u32[]{:S(2)}, u32[]{:S(2)}) collective-permute-start(bf16[2,3,8,1,32,128]{5,4,3,2,1,0:T(8,128)(2,1)S(1)} %slice.212), channel_id=1, source_target_pairs={{0,7},{1,0},{2,1},{3,2},{4,3},{5,4},{6,5},{7,6},{8,15},{9,8},{10,9... | collective-permute-start | bytes 1179656 | tf_op jit(solution)/shard_map/ppermute | solution.py:11
  17.1 1.1 copy-start.1
  17.1 1.2 copy-start.2
  17.1 2.1 %slice-start = ((bf16[2,3,8,8,32,128]{5,4,3,2,1,0:T(8,128)(2,1)}), bf16[2,3,7,8,32,128]{5,4,3,2,1,0:T(8,128)(2,1)S(1)}, s32[]{:S(2)}) async-start(bf16[2,3,8,8,32,128]{5,4,3,2,1,0:T(8,128)(2,1)} %param.3), calls=%async_computation.2 | async-start | bytes 5505024 | tf_op jit(solution)/shard_map/slice | solution.py:52
  41.3 119.0 %all-reduce.5.cloned.1.call-start = ((), (), s32[]{:S(2)}) async-start(), calls=%async_computation.1 | async-start | bytes 524288 | tf_op jit(solution)/shard_map/psum | solution.py:59
Sparse Core Ops, SparseCore 0:
  41.5 71.9 all-reduce.2
  116.3 44.0 all-reduce.4
